TPU v7x, 512 devices: a whole 4x8x8 slice. The times are simulated.
512 devices in a mesh: gx: 32 (over x, y), gy: 16 (over z, core).
Axes of the slice: x: 4, y: 8, z: 8, core: 2. Of those that a mesh axis runs over, the one named last changes fastest.
Arguments:
- test_block: float32 [32, 8, 512, 2048], P(None, None, 'gx', 'gy'), may hold values from -1500 to 1500, as said below
- kappa_sq: float32 [8, 512, 2048], P(None, 'gx', 'gy'), may hold values from 0.05 to 2
Outputs:
- basis: float32 [32, 8, 512, 2048], P(None, None, 'gx', 'gy')
Inputs may be any that keep to these rules, and one draw needn't show every extreme that they name: `test_block`: real-valued entries.
All inputs are finite; a program needn't handle non-finite values.
Results may differ from a plain program's by a relative error of at most 0.0003.
Values sent between devices are 32-bit elements; how exact they have to be, the bound alone decides.
No kernel may reach another device: no remote copies, remote signals or barrier semaphores. Data moves between devices by JAX's collectives and lax.ppermute only.
A program may use at most 64 MiB of HBM per device.

v0:
```python
import math
import jax
import jax.numpy as jnp
from jax import lax
from jax.sharding import PartitionSpec as P


def extended(block, sides, width):
    for axis, dim in sides:
        count = lax.axis_size(axis)
        forward = [(i, i + 1) for i in range(count - 1)]
        backward = [(target, source) for source, target in forward]
        low = lax.ppermute(
            lax.slice_in_dim(block, block.shape[dim] - width, None, axis=dim), axis, forward
        )
        high = lax.ppermute(lax.slice_in_dim(block, 0, width, axis=dim), axis, backward)
        block = jnp.concatenate([low, block, high], axis=dim)
    return block


def stencil(padded, coefficient):
    center = padded[:, :, 1:-1, 1:-1]
    neighbours = padded[:, :, 2:, 1:-1] + padded[:, :, :-2, 1:-1]
    neighbours = neighbours + padded[:, :, 1:-1, 2:] + padded[:, :, 1:-1, :-2]
    z_padded = jnp.pad(center, ((0, 0), (1, 1), (0, 0), (0, 0)))
    neighbours = neighbours + z_padded[:, 2:] + z_padded[:, :-2]
    return (6.0 + coefficient) * center - neighbours


def lower_solve(factor, block):
    return lax.linalg.triangular_solve(factor, block, left_side=True, lower=True)


def apply_once(field_in, kappa_sq):
    padded = extended(field_in, (("gx", 2), ("gy", 3)), 1)
    return stencil(padded, kappa_sq)


def merge_factors(stacked):
    summed = jnp.einsum("nij,nkj->ik", stacked, stacked, precision=lax.Precision.HIGHEST)
    return jnp.linalg.cholesky(summed)


def merged_factor(gram_matrix):
    stacked = lax.all_gather(gram_matrix[None], "gx", axis=0, tiled=True)
    column_factor = jnp.linalg.cholesky(jnp.sum(stacked, axis=0))
    stacked_columns = lax.all_gather(column_factor[None], "gy", axis=0, tiled=True)
    return merge_factors(stacked_columns)


def body(test_block, kappa_sq):
    cols_here, depth_here, x_cells, y_cells = test_block.shape
    sample = apply_once(apply_once(test_block, kappa_sq), kappa_sq)
    flattened = sample.reshape(cols_here, -1)
    gram_one = jnp.dot(flattened, flattened.T, precision=lax.Precision.HIGHEST)
    factor_one = merged_factor(gram_one)
    partial_value = lower_solve(factor_one, flattened)
    gram_two = jnp.dot(partial_value, partial_value.T, precision=lax.Precision.HIGHEST)
    factor_two = merged_factor(gram_two)
    scale_factor = math.sqrt(flattened.shape[1] * lax.axis_size("gx") * lax.axis_size("gy"))
    result = lower_solve(factor_two, partial_value) * scale_factor
    return result.reshape(cols_here, depth_here, x_cells, y_cells)


def solution(mesh):
    in_specs = (P(None, None, "gx", "gy"), P(None, "gx", "gy"))
    out_specs = P(None, None, "gx", "gy")
    return jax.shard_map(body, mesh=mesh, in_specs=in_specs, out_specs=out_specs, check_vma=False)
```

profile of v0, /device:TPU:1, one launch (start us, length us, event | category | flops | bytes accessed | tf_op | source)
XLA Modules:
  0.0 260.5 jit_solution(14732550015322631781)
XLA Ops:
  0.0 2.6 %copy.82 = f32[32,8,16,128]{3,1,2,0:T(8,128)S(1)} copy(f32[32,8,16,128]{3,2,1,0:T(8,128)} %param.5) | data formatting | bytes 4194304 | tf_op args[0]
  4.0 4.0 %collective-permute-start.1 = (f32[32,8,1,128]{3,1,2,0:T(8,128)S(1)}, f32[32,8,1,128]{3,1,2,0:T(8,128)S(1)}, u32[]{:S(2)}, u32[]{:S(2)}) collective-permute-start(f32[32,8,1,128]{3,1,2,0:T(8,128)S(1)} %get-tuple-element.13), channel_id=1, source_target_pairs={{0,16},{16,32},{32,48},{48,64},{64,80},{80,96},{96,112},{112,128},... | collective-permute-start | bytes 393224 | tf_op jit(solution)/shard_map/ppermute | solution.py:13
  9.3 4.5 %copy.88 = f32[32,8,16,128]{0,1,3,2:T(8,128)} copy(f32[32,8,16,128]{3,2,1,0:T(8,128)S(1)} %copy-done.2) | data formatting | bytes 4194304 | tf_op args[0]
  14.4 3.9 %pad_maximum_fusion = f32[32,8,18,128]{0,1,3,2:T(8,128)S(1)} fusion(f32[32,8,1,128]{0,1,3,2:T(8,128)S(1)} %copy.89, f32[32,8,16,128]{0,1,3,2:T(8,128)} %copy.88, f32[32,8,1,128]{0,1,3,2:T(8,128)S(1)} %copy.87), kind=kLoop, calls=%fused_computation.1 | loop fusion | flops 1179648 | bytes 4718592 | tf_op jit(solution)/shard_map/concatenate | solution.py:17
  18.4 3.6 %copy-done = f32[32,8,18,128]{0,1,3,2:T(8,128)} copy-done((f32[32,8,18,128]{0,1,3,2:T(8,128)}, f32[32,8,18,128]{0,1,3,2:T(8,128)S(1)}, u32[]{:S(2)}) %copy-start) | copy-done | bytes 2359320
  22.0 6.8 %collective-permute-start.2 = (f32[32,8,18,1]{0,1,3,2:T(8,128)S(1)}, f32[32,8,18,1]{0,1,3,2:T(8,128)S(1)}, u32[]{:S(2)}, u32[]{:S(2)}) collective-permute-start(f32[32,8,18,1]{0,1,3,2:T(8,128)S(1)} %get-tuple-element.6), channel_id=1, source_target_pairs={{1,0},{2,1},{3,2},{4,3},{5,4},{6,5},{7,6},{8,7},{9,8},{10,9},{11,1... | collective-permute-start | bytes 55304 | tf_op jit(solution)/shard_map/ppermute | solution.py:16
  30.7 7.9 %copy.90 = f32[32,8,18,128]{3,1,2,0:T(8,128)} copy(f32[32,8,18,128]{0,1,3,2:T(8,128)} %copy-done) | data formatting | bytes 4718592 | tf_op jit(solution)/shard_map/concatenate | solution.py:17
  43.3 8.0 %fusion.2 = f32[32,8,16,128]{3,1,2,0:T(8,128)S(1)} fusion(f32[32,8,16,128]{3,1,2,0:T(8,128)} %copy-done.1, f32[32,8,18,128]{3,1,2,0:T(8,128)} %copy.90, f32[32,8,18,1]{3,1,2,0:T(8,128)} %copy.92, f32[32,8,18,1]{3,1,2,0:T(8,128)} %copy.91, f32[32,8,1,128]{3,1,2,0:T(8,128)S(1)} %collective-permute-done.1, f32[32,8,1,128]{3,1,2,0:T(8,128)S(1)} %collective-permute-done, ...), kind=kLoop, calls=%fused_computation.9 | loop fusion | flops 5767168 | bytes 6918144 | tf_op jit(solution)/shard_map/sub | solution.py:27
  52.7 4.2 %collective-permute-start.5 = (f32[32,8,1,128]{3,1,2,0:T(8,128)S(1)}, f32[32,8,1,128]{3,1,2,0:T(8,128)S(1)}, u32[]{:S(2)}, u32[]{:S(2)}) collective-permute-start(f32[32,8,1,128]{3,1,2,0:T(8,128)S(1)} %get-tuple-element.11), channel_id=1, source_target_pairs={{0,16},{16,32},{32,48},{48,64},{64,80},{80,96},{96,112},{112,128},... | collective-permute-start | bytes 393224 | tf_op jit(solution)/shard_map/ppermute | solution.py:13
  59.2 2.9 %fusion.38 = (f32[32,8,18,1]{3,1,2,0:T(8,128)}, f32[32,8,18,1]{3,1,2,0:T(8,128)}) fusion(f32[32,8,18,128]{3,1,2,0:T(8,128)S(1)} %pad_maximum_fusion.1), kind=kLoop, calls=%fused_computation.71 | loop fusion | bytes 73728 | tf_op jit(solution)/shard_map/slice | solution.py:16
  62.1 2.6 copy.107
  64.7 3.4 %collective-permute-start.6 = (f32[32,8,18,1]{0,1,3,2:T(8,128)S(1)}, f32[32,8,18,1]{0,1,3,2:T(8,128)S(1)}, u32[]{:S(2)}, u32[]{:S(2)}) collective-permute-start(f32[32,8,18,1]{0,1,3,2:T(8,128)S(1)} %copy.107), channel_id=1, source_target_pairs={{1,0},{2,1},{3,2},{4,3},{5,4},{6,5},{7,6},{8,7},{9,8},{10,9},{11,1... | collective-permute-start | bytes 55304 | tf_op jit(solution)/shard_map/ppermute | solution.py:16
  68.1 2.6 copy.108
  77.7 4.0 %fusion.5 = f32[32,8,16,128]{3,1,2,0:T(8,128)S(1)} fusion(f32[32,8,16,128]{3,1,2,0:T(8,128)S(1)} %fusion.2, f32[32,8,18,1]{3,1,2,0:T(8,128)} %copy.98, f32[32,8,1,128]{3,1,2,0:T(8,128)S(1)} %collective-permute-done.4, f32[32,8,1,128]{3,1,2,0:T(8,128)S(1)} %collective-permute-done.5, f32[32,8,18,1]{3,1,2,0:T(8,128)} %copy.96, f32[8,16,128]{2,0,1:T(8,128)S(1)} %copy.81), kind=kLoop, calls=%fused_computation.12 | loop fusion | flops 7864320 | bytes 4558848 | tf_op jit(solution)/shard_map/sub | solution.py:27
  81.8 2.8 %fusion.18 = f32[32,32]{1,0:T(8,128)S(1)} fusion(f32[32,8,16,128]{3,1,2,0:T(8,128)S(1)} %fusion.5), kind=kOutput, calls=%fused_computation.37 | convolution fusion | flops 201326592 | bytes 2101248 | tf_op jit(solution)/shard_map/dot_general | solution.py:55
  86.3 43.5 %all-gather = f32[1024,32]{1,0:T(8,128)S(1)} all-gather(f32[32,32]{1,0:T(8,128)S(1)} %fusion.18), channel_id=2, replica_groups=mesh['gx'=32,'gy'=16] {'gx'}, dimensions={0}, use_global_device_ids=true | all-gather | bytes 135168 | tf_op jit(solution)/shard_map/all_gather | solution.py:45
  130.0 2.9 %cholesky.74 = f32[32,32]{1,0:T(8,128)S(1)} custom-call(f32[32,32]{1,0:T(8,128)S(1)} %fusion.28), custom_call_target="Cholesky" | custom-call | tf_op jit(solution)/shard_map/jit(cholesky)/cholesky | solution.py:46
  134.3 35.5 %all-gather.1 = f32[512,32]{1,0:T(8,128)S(1)} all-gather(f32[32,32]{1,0:T(8,128)S(1)} %fusion.30), channel_id=3, replica_groups=mesh['gx'=32,'gy'=16] {'gy'}, dimensions={0}, use_global_device_ids=true | all-gather | bytes 69632 | tf_op jit(solution)/shard_map/all_gather | solution.py:47
  170.2 2.9 %cholesky.85 = f32[32,32]{1,0:T(8,128)S(1)} custom-call(f32[32,32]{1,0:T(8,128)S(1)} %fusion.27), custom_call_target="Cholesky" | custom-call | tf_op jit(solution)/shard_map/jit(cholesky)/cholesky | solution.py:41
  177.0 4.6 %fusion.6 = f32[32,16384]{1,0:T(8,128)S(1)} fusion(f32[4,8,128,128]{3,2,1,0:T(8,128)} %bitcast.54, f32[1,32,32]{1,2,0:T(8,128)S(1)} %custom-call.6), kind=kOutput, calls=%fused_computation.13 | convolution fusion | flops 201326592 | bytes 4198400 | tf_op jit(solution)/shard_map/triangular_solve/dot.1 | solution.py:31
  183.4 35.5 %all-gather.2 = f32[1024,32]{1,0:T(8,128)S(1)} all-gather(f32[32,32]{1,0:T(8,128)S(1)} %fusion.41), channel_id=4, replica_groups=mesh['gx'=32,'gy'=16] {'gx'}, dimensions={0}, use_global_device_ids=true | all-gather | bytes 135168 | tf_op jit(solution)/shard_map/all_gather | solution.py:45
  219.1 2.9 %cholesky.96 = f32[32,32]{1,0:T(8,128)S(1)} custom-call(f32[32,32]{1,0:T(8,128)S(1)} %fusion.25), custom_call_target="Cholesky" | custom-call | tf_op jit(solution)/shard_map/jit(cholesky)/cholesky | solution.py:46
  223.3 26.4 %all-gather.3 = f32[512,32]{1,0:T(8,128)S(1)} all-gather(f32[32,32]{1,0:T(8,128)S(1)} %fusion.29), channel_id=5, replica_groups=mesh['gx'=32,'gy'=16] {'gy'}, dimensions={0}, use_global_device_ids=true | all-gather | bytes 69632 | tf_op jit(solution)/shard_map/all_gather | solution.py:47
  250.2 2.9 %cholesky.107 = f32[32,32]{1,0:T(8,128)S(1)} custom-call(f32[32,32]{1,0:T(8,128)S(1)} %fusion.24), custom_call_target="Cholesky" | custom-call | tf_op jit(solution)/shard_map/jit(cholesky)/cholesky | solution.py:41
  (61 shorter events, 39.1 us)
Async XLA Ops:
  0.0 9.3 %copy-start.2 = (f32[32,8,16,128]{3,2,1,0:T(8,128)S(1)}, f32[32,8,16,128]{3,2,1,0:T(8,128)}, u32[]{:S(2)}) copy-start(f32[32,8,16,128]{3,2,1,0:T(8,128)} %param.5) | copy-start | bytes 6291460
  2.6 1.3 copy-start.1
  4.0 9.9 %collective-permute-start.1 = (f32[32,8,1,128]{3,1,2,0:T(8,128)S(1)}, f32[32,8,1,128]{3,1,2,0:T(8,128)S(1)}, u32[]{:S(2)}, u32[]{:S(2)}) collective-permute-start(f32[32,8,1,128]{3,1,2,0:T(8,128)S(1)} %get-tuple-element.13), channel_id=1, source_target_pairs={{0,16},{16,32},{32,48},{48,64},{64,80},{80,96},{96,112},{112,128},... | collective-permute-start | bytes 393224 | tf_op jit(solution)/shard_map/ppermute | solution.py:13
  8.0 6.1 %collective-permute-start = (f32[32,8,1,128]{3,1,2,0:T(8,128)S(1)}, f32[32,8,1,128]{3,1,2,0:T(8,128)S(1)}, u32[]{:S(2)}, u32[]{:S(2)}) collective-permute-start(f32[32,8,1,128]{3,1,2,0:T(8,128)S(1)} %get-tuple-element.14), channel_id=1, source_target_pairs={{16,0},{32,16},{48,32},{64,48},{80,64},{96,80},{112,96},{128,112},... | collective-permute-start | bytes 393224 | tf_op jit(solution)/shard_map/ppermute | solution.py:16
  14.4 16.3 %copy-start.3 = (f32[8,16,128]{2,1,0:T(8,128)S(1)}, f32[8,16,128]{2,1,0:T(8,128)}, u32[]{:S(2)}) copy-start(f32[8,16,128]{2,1,0:T(8,128)} %param.6) | copy-start | bytes 196612
  18.3 3.6 %copy-start = (f32[32,8,18,128]{0,1,3,2:T(8,128)}, f32[32,8,18,128]{0,1,3,2:T(8,128)S(1)}, u32[]{:S(2)}) copy-start(f32[32,8,18,128]{0,1,3,2:T(8,128)S(1)} %pad_maximum_fusion) | copy-start | bytes 7077892
  22.0 16.7 %collective-permute-start.2 = (f32[32,8,18,1]{0,1,3,2:T(8,128)S(1)}, f32[32,8,18,1]{0,1,3,2:T(8,128)S(1)}, u32[]{:S(2)}, u32[]{:S(2)}) collective-permute-start(f32[32,8,18,1]{0,1,3,2:T(8,128)S(1)} %get-tuple-element.6), channel_id=1, source_target_pairs={{1,0},{2,1},{3,2},{4,3},{5,4},{6,5},{7,6},{8,7},{9,8},{10,9},{11,1... | collective-permute-start | bytes 55304 | tf_op jit(solution)/shard_map/ppermute | solution.py:16
  28.7 12.3 %collective-permute-start.3 = (f32[32,8,18,1]{0,1,3,2:T(8,128)S(1)}, f32[32,8,18,1]{0,1,3,2:T(8,128)S(1)}, u32[]{:S(2)}, u32[]{:S(2)}) collective-permute-start(f32[32,8,18,1]{0,1,3,2:T(8,128)S(1)} %get-tuple-element.8), channel_id=1, source_target_pairs={{0,1},{1,2},{2,3},{3,4},{4,5},{5,6},{6,7},{7,8},{8,9},{9,10},{10,1... | collective-permute-start | bytes 55304 | tf_op jit(solution)/shard_map/ppermute | solution.py:13
  51.4 6.8 %collective-permute-start.4 = (f32[32,8,1,128]{3,1,2,0:T(8,128)S(1)}, f32[32,8,1,128]{3,1,2,0:T(8,128)S(1)}, u32[]{:S(2)}, u32[]{:S(2)}) collective-permute-start(f32[32,8,1,128]{3,1,2,0:T(8,128)S(1)} %get-tuple-element.12), channel_id=1, source_target_pairs={{16,0},{32,16},{48,32},{64,48},{80,64},{96,80},{112,96},{128,112},... | collective-permute-start | bytes 393224 | tf_op jit(solution)/shard_map/ppermute | solution.py:16
  52.7 6.4 %collective-permute-start.5 = (f32[32,8,1,128]{3,1,2,0:T(8,128)S(1)}, f32[32,8,1,128]{3,1,2,0:T(8,128)S(1)}, u32[]{:S(2)}, u32[]{:S(2)}) collective-permute-start(f32[32,8,1,128]{3,1,2,0:T(8,128)S(1)} %get-tuple-element.11), channel_id=1, source_target_pairs={{0,16},{16,32},{32,48},{48,64},{64,80},{80,96},{96,112},{112,128},... | collective-permute-start | bytes 393224 | tf_op jit(solution)/shard_map/ppermute | solution.py:13
  64.7 8.3 %collective-permute-start.6 = (f32[32,8,18,1]{0,1,3,2:T(8,128)S(1)}, f32[32,8,18,1]{0,1,3,2:T(8,128)S(1)}, u32[]{:S(2)}, u32[]{:S(2)}) collective-permute-start(f32[32,8,18,1]{0,1,3,2:T(8,128)S(1)} %copy.107), channel_id=1, source_target_pairs={{1,0},{2,1},{3,2},{4,3},{5,4},{6,5},{7,6},{8,7},{9,8},{10,9},{11,1... | collective-permute-start | bytes 55304 | tf_op jit(solution)/shard_map/ppermute | solution.py:16
  70.7 4.7 %collective-permute-start.7 = (f32[32,8,18,1]{0,1,3,2:T(8,128)S(1)}, f32[32,8,18,1]{0,1,3,2:T(8,128)S(1)}, u32[]{:S(2)}, u32[]{:S(2)}) collective-permute-start(f32[32,8,18,1]{0,1,3,2:T(8,128)S(1)} %copy.108), channel_id=1, source_target_pairs={{0,1},{1,2},{2,3},{3,4},{4,5},{5,6},{6,7},{7,8},{8,9},{9,10},{10,1... | collective-permute-start | bytes 55304 | tf_op jit(solution)/shard_map/ppermute | solution.py:13
where the time goes:
time: 261 us
  blocking collectives  141 us (54%)
  local copies, waits for them, and re-layouts  41.7 us (16%)
  other arithmetic  38.4 us (15%)
  starting transfers between devices  25.2 us (10%)
  matrix products  11.8 us (5%)
    all_gather x2, blocking collectives, merged_factor(): stacked = lax.all_gather(gram_matrix[None], 'gx', axis=0, tiled=True)  79 us
    all_gather x2, blocking collectives, merged_factor(): lax.all_gather(column_factor[None], 'gy', axis=0, tiled=True)  61.9 us
    unnamed x13, local copies, waits for them, and re-layouts  19 us
    ppermute x4, starting transfers between devices, extended(): lax.ppermute(lax.slice_in_dim(block, 0, width, axis=dim), axis, backward)  12.7 us
    ppermute x4, starting transfers between devices, extended(): lax.ppermute(lax.slice_in_dim(block, block.shape[dim] - width, None, axis...  12.5 us
    sub x2, other arithmetic, stencil(): return (6.0 + coefficient) * center - neighbours  12 us
    concatenate x1, local copies, waits for them, and re-layouts, extended(): block = jnp.concatenate([low, block, high], axis=dim)  7.95 us
    another operation x6, other arithmetic, merged_factor(): column_factor = jnp.linalg.cholesky(jnp.sum(stacked, axis=0))  7.27 us
  transfers between devices with their start and end apart: 8, of which 2 were waited for; matrix products, arithmetic and copies ran while one was open for 8% of the time, Pallas kernels for 0%

commit v1 on v0

--- a/solution.py
+++ b/solution.py
@@ -3,6 +3,13 @@
 import jax.numpy as jnp
 from jax import lax
 from jax.sharding import PartitionSpec as P
+
+
+def all_by_exchange(shard, mesh_axis, dim):
+    peers = lax.axis_size(mesh_axis)
+    pieces = jnp.stack([shard for _ in range(peers)])
+    pieces = lax.all_to_all(pieces, mesh_axis, split_axis=0, concat_axis=0)
+    return jnp.concatenate(pieces, axis=dim)
 
 
 def extended(block, sides, width):
@@ -42,7 +49,7 @@
 
 
 def merged_factor(gram_matrix):
-    stacked = lax.all_gather(gram_matrix[None], "gx", axis=0, tiled=True)
+    stacked = all_by_exchange(gram_matrix[None], "gx", 0)
     column_factor = jnp.linalg.cholesky(jnp.sum(stacked, axis=0))
     stacked_columns = lax.all_gather(column_factor[None], "gy", axis=0, tiled=True)
     return merge_factors(stacked_columns)

time: 261 us -> 200 us (0.77)
  blocking collectives: 141 us -> 53.6 us
  starting transfers between devices: 25.2 us -> 38.2 us
  waiting for transfers between devices: 2.24 us -> 8.95 us
  local copies, waits for them, and re-layouts: 41.7 us -> 46.7 us
    all_gather x2 -> x0, blocking collectives: 79 us -> none  [merged_factor(): stacked = lax.all_gather(gram_matrix[None], 'gx', axis=0, tiled=True)]
    all_gather x2, blocking collectives: 61.9 us -> 41.2 us  [merged_factor(): lax.all_gather(column_factor[None], 'gy', axis=0, tiled=True)]
    all_to_all x0 -> x1, starting transfers between devices: none -> 13.1 us  [all_by_exchange(): pieces = lax.all_to_all(pieces, mesh_axis, split_axis=0, concat_axis=0)]
    all_to_all x0 -> x1, blocking collectives: none -> 12.4 us  [all_by_exchange(): pieces = lax.all_to_all(pieces, mesh_axis, split_axis=0, concat_axis=0)]
    all_to_all x0 -> x1, waiting for transfers between devices: none -> 6.71 us  [all_by_exchange(): pieces = lax.all_to_all(pieces, mesh_axis, split_axis=0, concat_axis=0)]
    unnamed x13 -> x19, local copies, waits for them, and re-layouts: 19 us -> 21.8 us
  transfers between devices with their start and end apart: 8 -> 9, of which waited for: 2 -> 3; matrix products, arithmetic and copies ran while one was open for 8% -> 12% of each run, Pallas kernels for 0% -> 0%
where the time goes in v1:
time: 200 us
  blocking collectives  53.6 us (27%)
  local copies, waits for them, and re-layouts  46.7 us (23%)
  other arithmetic  40 us (20%)
  starting transfers between devices  38.2 us (19%)
  matrix products  11.8 us (6%)
  waiting for transfers between devices  8.95 us (4%)
    all_gather x2, blocking collectives, merged_factor(): lax.all_gather(column_factor[None], 'gy', axis=0, tiled=True)  41.2 us
    unnamed x19, local copies, waits for them, and re-layouts  21.8 us
    all_to_all x1, starting transfers between devices, all_by_exchange(): pieces = lax.all_to_all(pieces, mesh_axis, split_axis=0, concat_axis=0)  13.1 us
    ppermute x4, starting transfers between devices, extended(): lax.ppermute(lax.slice_in_dim(block, 0, width, axis=dim), axis, backward)  12.7 us
    ppermute x4, starting transfers between devices, extended(): lax.ppermute(lax.slice_in_dim(block, block.shape[dim] - width, None, axis...  12.5 us
    all_to_all x1, blocking collectives, all_by_exchange(): pieces = lax.all_to_all(pieces, mesh_axis, split_axis=0, concat_axis=0)  12.4 us
    sub x2, other arithmetic, stencil(): return (6.0 + coefficient) * center - neighbours  12 us
    concatenate x1, local copies, waits for them, and re-layouts, extended(): block = jnp.concatenate([low, block, high], axis=dim)  7.95 us
  transfers between devices with their start and end apart: 9, of which 3 were waited for; matrix products, arithmetic and copies ran while one was open for 12% of the time, Pallas kernels for 0%

profile of v1, /device:TPU:1, one launch (start us, length us, event | category | flops | bytes accessed | tf_op | source)
XLA Modules:
  0.0 199.7 jit_solution(16346007854412705644)
XLA Ops:
  0.0 2.6 %copy.82 = f32[32,8,16,128]{3,1,2,0:T(8,128)S(1)} copy(f32[32,8,16,128]{3,2,1,0:T(8,128)} %param.5) | data formatting | bytes 4194304 | tf_op args[0]
  4.0 4.0 %collective-permute-start.1 = (f32[32,8,1,128]{3,1,2,0:T(8,128)S(1)}, f32[32,8,1,128]{3,1,2,0:T(8,128)S(1)}, u32[]{:S(2)}, u32[]{:S(2)}) collective-permute-start(f32[32,8,1,128]{3,1,2,0:T(8,128)S(1)} %get-tuple-element.13), channel_id=1, source_target_pairs={{0,16},{16,32},{32,48},{48,64},{64,80},{80,96},{96,112},{112,128},... | collective-permute-start | bytes 393224 | tf_op jit(solution)/shard_map/ppermute | solution.py:20
  9.3 4.5 %copy.88 = f32[32,8,16,128]{0,1,3,2:T(8,128)} copy(f32[32,8,16,128]{3,2,1,0:T(8,128)S(1)} %copy-done.3) | data formatting | bytes 4194304 | tf_op args[0]
  14.4 3.9 %pad_maximum_fusion = f32[32,8,18,128]{0,1,3,2:T(8,128)S(1)} fusion(f32[32,8,1,128]{0,1,3,2:T(8,128)S(1)} %copy.89, f32[32,8,16,128]{0,1,3,2:T(8,128)} %copy.88, f32[32,8,1,128]{0,1,3,2:T(8,128)S(1)} %copy.87), kind=kLoop, calls=%fused_computation.1 | loop fusion | flops 1179648 | bytes 4718592 | tf_op jit(solution)/shard_map/concatenate | solution.py:24
  18.4 3.6 %copy-done = f32[32,8,18,128]{0,1,3,2:T(8,128)} copy-done((f32[32,8,18,128]{0,1,3,2:T(8,128)}, f32[32,8,18,128]{0,1,3,2:T(8,128)S(1)}, u32[]{:S(2)}) %copy-start) | copy-done | bytes 2359320
  22.0 6.8 %collective-permute-start.2 = (f32[32,8,18,1]{0,1,3,2:T(8,128)S(1)}, f32[32,8,18,1]{0,1,3,2:T(8,128)S(1)}, u32[]{:S(2)}, u32[]{:S(2)}) collective-permute-start(f32[32,8,18,1]{0,1,3,2:T(8,128)S(1)} %get-tuple-element.6), channel_id=1, source_target_pairs={{1,0},{2,1},{3,2},{4,3},{5,4},{6,5},{7,6},{8,7},{9,8},{10,9},{11,1... | collective-permute-start | bytes 55304 | tf_op jit(solution)/shard_map/ppermute | solution.py:23
  30.7 7.9 %copy.90 = f32[32,8,18,128]{3,1,2,0:T(8,128)} copy(f32[32,8,18,128]{0,1,3,2:T(8,128)} %copy-done) | data formatting | bytes 4718592 | tf_op jit(solution)/shard_map/concatenate | solution.py:24
  43.3 8.0 %fusion.2 = f32[32,8,16,128]{3,1,2,0:T(8,128)S(1)} fusion(f32[32,8,16,128]{3,1,2,0:T(8,128)} %copy-done.2, f32[32,8,18,128]{3,1,2,0:T(8,128)} %copy.90, f32[32,8,18,1]{3,1,2,0:T(8,128)} %copy.92, f32[32,8,18,1]{3,1,2,0:T(8,128)} %copy.91, f32[32,8,1,128]{3,1,2,0:T(8,128)S(1)} %collective-permute-done.1, f32[32,8,1,128]{3,1,2,0:T(8,128)S(1)} %collective-permute-done, ...), kind=kLoop, calls=%fused_computation.9 | loop fusion | flops 5767168 | bytes 6918144 | tf_op jit(solution)/shard_map/sub | solution.py:34
  52.7 4.2 %collective-permute-start.5 = (f32[32,8,1,128]{3,1,2,0:T(8,128)S(1)}, f32[32,8,1,128]{3,1,2,0:T(8,128)S(1)}, u32[]{:S(2)}, u32[]{:S(2)}) collective-permute-start(f32[32,8,1,128]{3,1,2,0:T(8,128)S(1)} %get-tuple-element.11), channel_id=1, source_target_pairs={{0,16},{16,32},{32,48},{48,64},{64,80},{80,96},{96,112},{112,128},... | collective-permute-start | bytes 393224 | tf_op jit(solution)/shard_map/ppermute | solution.py:20
  59.2 2.9 %fusion.38 = (f32[32,8,18,1]{3,1,2,0:T(8,128)}, f32[32,8,18,1]{3,1,2,0:T(8,128)}) fusion(f32[32,8,18,128]{3,1,2,0:T(8,128)S(1)} %pad_maximum_fusion.1), kind=kLoop, calls=%fused_computation.71 | loop fusion | bytes 73728 | tf_op jit(solution)/shard_map/slice | solution.py:23
  64.7 3.4 %collective-permute-start.6 = (f32[32,8,18,1]{0,1,3,2:T(8,128)S(1)}, f32[32,8,18,1]{0,1,3,2:T(8,128)S(1)}, u32[]{:S(2)}, u32[]{:S(2)}) collective-permute-start(f32[32,8,18,1]{0,1,3,2:T(8,128)S(1)} %copy.107), channel_id=1, source_target_pairs={{1,0},{2,1},{3,2},{4,3},{5,4},{6,5},{7,6},{8,7},{9,8},{10,9},{11,1... | collective-permute-start | bytes 55304 | tf_op jit(solution)/shard_map/ppermute | solution.py:23
  77.7 4.0 %fusion.5 = f32[32,8,16,128]{3,1,2,0:T(8,128)S(1)} fusion(f32[32,8,16,128]{3,1,2,0:T(8,128)S(1)} %fusion.2, f32[32,8,18,1]{3,1,2,0:T(8,128)} %copy.98, f32[32,8,1,128]{3,1,2,0:T(8,128)S(1)} %collective-permute-done.4, f32[32,8,1,128]{3,1,2,0:T(8,128)S(1)} %collective-permute-done.5, f32[32,8,18,1]{3,1,2,0:T(8,128)} %copy.96, f32[8,16,128]{2,0,1:T(8,128)S(1)} %copy.81), kind=kLoop, calls=%fused_computation.12 | loop fusion | flops 7864320 | bytes 4558848 | tf_op jit(solution)/shard_map/sub | solution.py:34
  83.1 2.8 %fusion.18 = f32[32,32]{1,0:T(8,128)S(1)} fusion(f32[32,8,16,128]{3,1,2,0:T(8,128)S(1)} %fusion.5), kind=kOutput, calls=%fused_computation.37 | convolution fusion | flops 201326592 | bytes 2101248 | tf_op jit(solution)/shard_map/dot_general | solution.py:62
  86.9 13.1 %all-to-all-start = ((f32[32,1,1024]{2,1,0:T(1,128)}), f32[32,1,1024]{2,1,0:T(1,128)S(1)}, u32[]{:S(2)}, u32[]{:S(2)}) async-start(f32[32,1,1024]{2,1,0:T(1,128)} %reshape.37), calls=%async_computation | async-start | bytes 262144 | tf_op jit(solution)/shard_map/all_to_all | solution.py:11
  100.0 3.3 %copy.103 = f32[32,8,16,128]{3,2,1,0:T(8,128)} copy(f32[32,8,16,128]{3,1,2,0:T(8,128)} %copy-done.1) | data formatting | bytes 4194304 | tf_op jit(solution)/shard_map/sub | solution.py:34
  103.3 6.7 %all-to-all-done = f32[32,1,1024]{2,1,0:T(1,128)S(1)} async-done(((f32[32,1,1024]{2,1,0:T(1,128)}), f32[32,1,1024]{2,1,0:T(1,128)S(1)}, u32[]{:S(2)}, u32[]{:S(2)}) %all-to-all-start) | async-done | bytes 131104 | tf_op jit(solution)/shard_map/all_to_all | solution.py:11
  111.8 2.9 %cholesky.74 = f32[32,32]{1,0:T(8,128)S(1)} custom-call(f32[32,32]{1,0:T(8,128)S(1)} %fusion.28), custom_call_target="Cholesky" | custom-call | tf_op jit(solution)/shard_map/jit(cholesky)/cholesky | solution.py:53
  116.0 24.4 %all-gather = f32[512,32]{1,0:T(8,128)S(1)} all-gather(f32[32,32]{1,0:T(8,128)S(1)} %fusion.30), channel_id=2, replica_groups=mesh['gx'=32,'gy'=16] {'gy'}, dimensions={0}, use_global_device_ids=true | all-gather | bytes 69632 | tf_op jit(solution)/shard_map/all_gather | solution.py:54
  140.8 2.9 %cholesky.85 = f32[32,32]{1,0:T(8,128)S(1)} custom-call(f32[32,32]{1,0:T(8,128)S(1)} %fusion.27), custom_call_target="Cholesky" | custom-call | tf_op jit(solution)/shard_map/jit(cholesky)/cholesky | solution.py:48
  147.5 4.6 %fusion.6 = f32[32,16384]{1,0:T(8,128)S(1)} fusion(f32[4,8,128,128]{3,2,1,0:T(8,128)} %bitcast.52, f32[1,32,32]{1,2,0:T(8,128)S(1)} %custom-call.6), kind=kOutput, calls=%fused_computation.13 | convolution fusion | flops 201326592 | bytes 4198400 | tf_op jit(solution)/shard_map/triangular_solve/dot.1 | solution.py:38
  154.2 12.4 %all_to_all.10 = f32[32,1,1024]{2,1,0:T(1,128)S(1)} all-to-all(f32[32,1,1024]{2,1,0:T(1,128)S(1)} %reshape.39), channel_id=1, replica_groups=mesh['gx'=32,'gy'=16] {'gx'}, dimensions={0} | all-to-all | bytes 262144 | tf_op jit(solution)/shard_map/all_to_all | solution.py:11
  167.9 2.9 %cholesky.96 = f32[32,32]{1,0:T(8,128)S(1)} custom-call(f32[32,32]{1,0:T(8,128)S(1)} %fusion.25), custom_call_target="Cholesky" | custom-call | tf_op jit(solution)/shard_map/jit(cholesky)/cholesky | solution.py:53
  172.1 16.8 %all-gather.1 = f32[512,32]{1,0:T(8,128)S(1)} all-gather(f32[32,32]{1,0:T(8,128)S(1)} %fusion.29), channel_id=3, replica_groups=mesh['gx'=32,'gy'=16] {'gy'}, dimensions={0}, use_global_device_ids=true | all-gather | bytes 69632 | tf_op jit(solution)/shard_map/all_gather | solution.py:54
  189.4 2.9 %cholesky.107 = f32[32,32]{1,0:T(8,128)S(1)} custom-call(f32[32,32]{1,0:T(8,128)S(1)} %fusion.24), custom_call_target="Cholesky" | custom-call | tf_op jit(solution)/shard_map/jit(cholesky)/cholesky | solution.py:48
  (73 shorter events, 47.7 us)
Async XLA Ops:
  0.0 9.3 %copy-start.3 = (f32[32,8,16,128]{3,2,1,0:T(8,128)S(1)}, f32[32,8,16,128]{3,2,1,0:T(8,128)}, u32[]{:S(2)}) copy-start(f32[32,8,16,128]{3,2,1,0:T(8,128)} %param.5) | copy-start | bytes 6291460
  2.6 1.3 copy-start.2
  4.0 9.9 %collective-permute-start.1 = (f32[32,8,1,128]{3,1,2,0:T(8,128)S(1)}, f32[32,8,1,128]{3,1,2,0:T(8,128)S(1)}, u32[]{:S(2)}, u32[]{:S(2)}) collective-permute-start(f32[32,8,1,128]{3,1,2,0:T(8,128)S(1)} %get-tuple-element.13), channel_id=1, source_target_pairs={{0,16},{16,32},{32,48},{48,64},{64,80},{80,96},{96,112},{112,128},... | collective-permute-start | bytes 393224 | tf_op jit(solution)/shard_map/ppermute | solution.py:20
  8.0 6.1 %collective-permute-start = (f32[32,8,1,128]{3,1,2,0:T(8,128)S(1)}, f32[32,8,1,128]{3,1,2,0:T(8,128)S(1)}, u32[]{:S(2)}, u32[]{:S(2)}) collective-permute-start(f32[32,8,1,128]{3,1,2,0:T(8,128)S(1)} %get-tuple-element.14), channel_id=1, source_target_pairs={{16,0},{32,16},{48,32},{64,48},{80,64},{96,80},{112,96},{128,112},... | collective-permute-start | bytes 393224 | tf_op jit(solution)/shard_map/ppermute | solution.py:23
  14.4 16.3 %copy-start.4 = (f32[8,16,128]{2,1,0:T(8,128)S(1)}, f32[8,16,128]{2,1,0:T(8,128)}, u32[]{:S(2)}) copy-start(f32[8,16,128]{2,1,0:T(8,128)} %param.6) | copy-start | bytes 196612
  18.3 3.6 %copy-start = (f32[32,8,18,128]{0,1,3,2:T(8,128)}, f32[32,8,18,128]{0,1,3,2:T(8,128)S(1)}, u32[]{:S(2)}) copy-start(f32[32,8,18,128]{0,1,3,2:T(8,128)S(1)} %pad_maximum_fusion) | copy-start | bytes 7077892
  22.0 16.7 %collective-permute-start.2 = (f32[32,8,18,1]{0,1,3,2:T(8,128)S(1)}, f32[32,8,18,1]{0,1,3,2:T(8,128)S(1)}, u32[]{:S(2)}, u32[]{:S(2)}) collective-permute-start(f32[32,8,18,1]{0,1,3,2:T(8,128)S(1)} %get-tuple-element.6), channel_id=1, source_target_pairs={{1,0},{2,1},{3,2},{4,3},{5,4},{6,5},{7,6},{8,7},{9,8},{10,9},{11,1... | collective-permute-start | bytes 55304 | tf_op jit(solution)/shard_map/ppermute | solution.py:23
  28.7 12.3 %collective-permute-start.3 = (f32[32,8,18,1]{0,1,3,2:T(8,128)S(1)}, f32[32,8,18,1]{0,1,3,2:T(8,128)S(1)}, u32[]{:S(2)}, u32[]{:S(2)}) collective-permute-start(f32[32,8,18,1]{0,1,3,2:T(8,128)S(1)} %get-tuple-element.8), channel_id=1, source_target_pairs={{0,1},{1,2},{2,3},{3,4},{4,5},{5,6},{6,7},{7,8},{8,9},{9,10},{10,1... | collective-permute-start | bytes 55304 | tf_op jit(solution)/shard_map/ppermute | solution.py:20
  51.4 6.8 %collective-permute-start.4 = (f32[32,8,1,128]{3,1,2,0:T(8,128)S(1)}, f32[32,8,1,128]{3,1,2,0:T(8,128)S(1)}, u32[]{:S(2)}, u32[]{:S(2)}) collective-permute-start(f32[32,8,1,128]{3,1,2,0:T(8,128)S(1)} %get-tuple-element.12), channel_id=1, source_target_pairs={{16,0},{32,16},{48,32},{64,48},{80,64},{96,80},{112,96},{128,112},... | collective-permute-start | bytes 393224 | tf_op jit(solution)/shard_map/ppermute | solution.py:23
  52.7 6.4 %collective-permute-start.5 = (f32[32,8,1,128]{3,1,2,0:T(8,128)S(1)}, f32[32,8,1,128]{3,1,2,0:T(8,128)S(1)}, u32[]{:S(2)}, u32[]{:S(2)}) collective-permute-start(f32[32,8,1,128]{3,1,2,0:T(8,128)S(1)} %get-tuple-element.11), channel_id=1, source_target_pairs={{0,16},{16,32},{32,48},{48,64},{64,80},{80,96},{96,112},{112,128},... | collective-permute-start | bytes 393224 | tf_op jit(solution)/shard_map/ppermute | solution.py:20
  64.7 8.3 %collective-permute-start.6 = (f32[32,8,18,1]{0,1,3,2:T(8,128)S(1)}, f32[32,8,18,1]{0,1,3,2:T(8,128)S(1)}, u32[]{:S(2)}, u32[]{:S(2)}) collective-permute-start(f32[32,8,18,1]{0,1,3,2:T(8,128)S(1)} %copy.107), channel_id=1, source_target_pairs={{1,0},{2,1},{3,2},{4,3},{5,4},{6,5},{7,6},{8,7},{9,8},{10,9},{11,1... | collective-permute-start | bytes 55304 | tf_op jit(solution)/shard_map/ppermute | solution.py:23
  70.7 4.7 %collective-permute-start.7 = (f32[32,8,18,1]{0,1,3,2:T(8,128)S(1)}, f32[32,8,18,1]{0,1,3,2:T(8,128)S(1)}, u32[]{:S(2)}, u32[]{:S(2)}) collective-permute-start(f32[32,8,18,1]{0,1,3,2:T(8,128)S(1)} %copy.108), channel_id=1, source_target_pairs={{0,1},{1,2},{2,3},{3,4},{4,5},{5,6},{6,7},{7,8},{8,9},{9,10},{10,1... | collective-permute-start | bytes 55304 | tf_op jit(solution)/shard_map/ppermute | solution.py:20
  81.8 1.3 copy-start.1
  86.9 23.1 %all-to-all-start = ((f32[32,1,1024]{2,1,0:T(1,128)}), f32[32,1,1024]{2,1,0:T(1,128)S(1)}, u32[]{:S(2)}, u32[]{:S(2)}) async-start(f32[32,1,1024]{2,1,0:T(1,128)} %reshape.37), calls=%async_computation | async-start | bytes 262144 | tf_op jit(solution)/shard_map/all_to_all | solution.py:11
